TPU v7x, 512 devices: a whole 4x8x8 slice. The times are simulated.
512 devices in a mesh: dp: 32 (over y, x), section: 4 (over z_hi), space: 4 (over z_lo, core).
Axes of the slice: x: 4, y: 8, z: 8 (z_hi: 4, z_lo: 2; z = z_hi * 2 + z_lo), core: 2. Of those that a mesh axis runs over, the one named last changes fastest.
Arguments:
- images: bfloat16 [64, 4, 64, 256], P('dp', 'space'), may hold values from -6 to 6
- steps: int32 [64], P('dp'), may hold values from 0 to 999
- out_grad: bfloat16 [64, 4, 64, 256], P('dp', 'space'), may hold values from -0.125 to 0.125
- conv_weight: bfloat16 [4, 3, 3, 256, 256], P('section'), may hold values from -0.125 to 0.125
- gn_gain: float32 [4, 256], P('section'), may hold values from 0.5 to 2
- emb_weight: bfloat16 [4, 256, 512], P('section'), may hold values from -0.375 to 0.375
Outputs:
- grad_conv: float32 [4, 3, 3, 256, 256], P('section')
- grad_gain: float32 [4, 256], P('section')
- grad_emb: float32 [4, 256, 512], P('section')
All inputs are finite; a program needn't handle non-finite values.
Results may differ from a plain program's by a relative error of at most 0.0064.
Values may be sent and summed in bfloat16 or wider, within the bound.
No kernel may reach another device: no remote copies, remote signals or barrier semaphores. Data moves between devices by JAX's collectives and lax.ppermute only.
A program may use at most 64 MiB of HBM per device.

v0:
```python
import math
import jax
import jax.numpy as jnp
from jax import lax
from jax.sharding import PartitionSpec as P

G = 32
FREQ = 256
MICRO = 2
EPS = 1e-05


def from_behind(value, axis, steps):
    count = lax.axis_size(axis)
    initial, last = (max(0, -steps), min(count, count - steps))
    return lax.ppermute(value, axis, [(source, source + steps) for source in range(initial, last)])


def extended(shard, sides, width):
    for axis, dim in sides:
        size, length = (lax.axis_size(axis), shard.shape[dim])
        up = [(i, (i + 1) % size) for i in range(size - 1)]
        down = [(j, i) for i, j in up]
        last = lax.slice_in_dim(shard, length - width, length, axis=dim)
        initial = lax.slice_in_dim(shard, 0, width, axis=dim)
        before = lax.ppermute(last, axis, up)
        after = lax.ppermute(initial, axis, down)
        shard = jnp.concatenate([before, shard, after], axis=dim)
    return shard


def sinusoid(timesteps, feature_n):
    half_n = feature_n // 2
    freqs = jnp.exp(-math.log(10000.0) * jnp.arange(half_n, dtype=jnp.float32) / half_n)
    angles = timesteps.astype(jnp.float32)[:, None] * freqs[None, :]
    return jnp.concatenate([jnp.cos(angles), jnp.sin(angles)], axis=1)


def group_sums(tensor, groups):
    batch_n, height_n, width_n, channels = tensor.shape
    split = tensor.reshape(batch_n, height_n, width_n, groups, channels // groups)
    return (jnp.sum(split, axis=(1, 2, 4)), jnp.sum(split * split, axis=(1, 2, 4)))


def spread(values, channels):
    return jnp.repeat(values, channels // values.shape[1], axis=1)[:, None, None, :]


def normalize(tensor, first_sum, square_sum, gains, scales, shifts, cell_count):
    channels = tensor.shape[3]
    average = first_sum / cell_count
    inverse = lax.rsqrt(square_sum / cell_count - average * average + EPS)
    normed = (tensor - spread(average, channels)) * spread(inverse, channels) * gains
    return normed * (1.0 + scales[:, None, None, :]) + shifts[:, None, None, :]


def patches(padded, height_n, width_n):
    return jnp.concatenate(
        [
            padded[:, vertical : vertical + height_n, lateral : lateral + width_n, :]
            for vertical in range(3)
            for lateral in range(3)
        ],
        axis=3,
    )


def convolve(padded, matrix):
    batch_n, height_p, width_p, channels = padded.shape
    flat = patches(padded, height_p - 2, width_p - 2).reshape(-1, 9 * channels)
    return jnp.dot(flat, matrix, preferred_element_type=jnp.float32).reshape(
        batch_n, height_p - 2, width_p - 2, matrix.shape[1]
    )


def flip_weight(weight):
    channels = weight.shape[2]
    return jnp.transpose(weight[::-1, ::-1], (0, 1, 3, 2)).reshape(9 * channels, channels)


def silu_slope(pre_act):
    sigmoid_v = jax.nn.sigmoid(pre_act)
    return sigmoid_v * (1.0 + pre_act * (1.0 - sigmoid_v))


def pad_columns(tensor):
    return jnp.pad(tensor, ((0, 0), (0, 0), (1, 1), (0, 0)))


def pick(stacked, index):
    return lax.dynamic_index_in_dim(stacked, index, 0, keepdims=False)


def norm_backward(tensor, first_sum, square_sum, gains, scales, shifts, cell_count, d_pre):

    def mapping(tensor_v, first_v, square_v, gains_v, scales_v, shifts_v):
        return normalize(tensor_v, first_v, square_v, gains_v, scales_v, shifts_v, cell_count)

    _, pull_back = jax.vjp(mapping, tensor, first_sum, square_sum, gains, scales, shifts)
    return pull_back(d_pre)


def per_device(images, steps, out_grad, conv_weight, gn_gain, emb_weight):
    section_count = lax.axis_size("section")
    tick_count = MICRO + section_count - 1
    section_no = lax.axis_index("section")
    local_n = images.shape[0] // MICRO
    row_count = images.shape[1]
    col_count = images.shape[2]
    channels = images.shape[3]
    cell_count = row_count * lax.axis_size("space") * col_count * (channels // G)
    weight = conv_weight[0]
    flat_weight = weight.reshape(9 * channels, channels)
    flipped = flip_weight(weight)
    gains = gn_gain[0]
    all_features = sinusoid(steps, FREQ)
    features = all_features.reshape(MICRO, local_n, FREQ)
    embedded = jnp.dot(
        all_features, emb_weight[0].astype(jnp.float32), precision=lax.Precision.HIGHEST
    ).reshape(MICRO, local_n, 2 * channels)
    batches = images.reshape(MICRO, local_n, row_count, col_count, channels)
    cotangents = out_grad.reshape(MICRO, local_n, row_count, col_count, channels)
    blank = jnp.zeros((local_n, row_count, col_count, channels), jnp.bfloat16)
    carried = blank
    skips = []
    kept_in = []
    kept_first = []
    kept_square = []
    kept_pad = []
    for moment in range(tick_count):
        arrived = blank
        if moment > 0:
            arrived = from_behind(carried, "section", 1)
        inputs = jnp.where(section_no == 0, batches[min(moment, MICRO - 1)], arrived)
        late = moment - (section_count - 1)
        if 0 <= late < MICRO:
            joined = (arrived.astype(jnp.float32) + skips[late].astype(jnp.float32)).astype(
                jnp.bfloat16
            )
            inputs = jnp.where(section_no == section_count - 1, joined, inputs)
        which = jnp.clip(moment - section_no, 0, MICRO - 1)
        chosen = pick(embedded, which)
        tensor = inputs.astype(jnp.float32)
        first_sum, square_sum = group_sums(tensor, G)
        first_sum, square_sum = lax.psum((first_sum, square_sum), "space")
        pre_act = normalize(
            tensor,
            first_sum,
            square_sum,
            gains,
            chosen[:, :channels],
            chosen[:, channels:],
            cell_count,
        )
        activation = jax.nn.silu(pre_act).astype(jnp.bfloat16)
        padded = pad_columns(extended(activation, (("space", 1),), 1))
        conv_out = convolve(padded, flat_weight)
        output = (tensor + conv_out).astype(jnp.bfloat16)
        if moment < MICRO:
            skips.append(from_behind(output, "section", section_count - 1))
        kept_in.append(inputs)
        kept_first.append(first_sum)
        kept_square.append(square_sum)
        kept_pad.append(padded)
        carried = output
    stack_in = jnp.stack(kept_in)
    stack_first = jnp.stack(kept_first)
    stack_square = jnp.stack(kept_square)
    stack_pad = jnp.stack(kept_pad)
    weight_grad = jnp.zeros((9 * channels, channels), jnp.float32)
    gain_grad = jnp.zeros((channels,), jnp.float32)
    emb_grad = jnp.zeros((FREQ, 2 * channels), jnp.float32)
    carried = blank
    skip_grads = []
    for moment in range(tick_count):
        arrived = blank
        if moment > 0:
            arrived = from_behind(carried, "section", -1)
        top_grad = cotangents[moment] if moment < MICRO else blank
        upstream = jnp.where(section_no == section_count - 1, top_grad, arrived)
        early = moment - (section_count - 1)
        if 0 <= early < MICRO:
            joined = (arrived.astype(jnp.float32) + skip_grads[early].astype(jnp.float32)).astype(
                jnp.bfloat16
            )
            upstream = jnp.where(section_no == 0, joined, upstream)
        which_raw = moment - (section_count - 1) + section_no
        valid = (which_raw >= 0) & (which_raw < MICRO)
        upstream = jnp.where(valid, upstream, blank)
        which = jnp.clip(which_raw, 0, MICRO - 1)
        forward_at = jnp.clip(which_raw + section_no, 0, tick_count - 1)
        tensor = pick(stack_in, forward_at).astype(jnp.float32)
        first_sum = pick(stack_first, forward_at)
        square_sum = pick(stack_square, forward_at)
        chosen = pick(embedded, which)
        scales = chosen[:, :channels]
        shifts = chosen[:, channels:]
        pre_act = normalize(tensor, first_sum, square_sum, gains, scales, shifts, cell_count)
        padded = pick(stack_pad, forward_at)
        flat_patch = patches(padded, row_count, col_count).reshape(-1, 9 * channels)
        weight_grad = weight_grad + jnp.dot(
            flat_patch.T, upstream.reshape(-1, channels), preferred_element_type=jnp.float32
        )
        up_pad = pad_columns(extended(upstream, (("space", 1),), 1))
        d_act = convolve(up_pad, flipped)
        d_pre = d_act * silu_slope(pre_act)
        d_tensor, d_first, d_square, d_gains, d_scales, d_shifts = norm_backward(
            tensor, first_sum, square_sum, gains, scales, shifts, cell_count, d_pre
        )
        d_first, d_square = lax.psum((d_first, d_square), "space")
        d_tensor = d_tensor + spread(d_first, channels) + 2.0 * tensor * spread(d_square, channels)
        d_input = (upstream.astype(jnp.float32) + d_tensor).astype(jnp.bfloat16)
        gain_grad = gain_grad + d_gains
        emb_grad = emb_grad + jnp.dot(
            pick(features, which).T,
            jnp.concatenate([d_scales, d_shifts], axis=1),
            precision=lax.Precision.HIGHEST,
        )
        if moment < MICRO:
            skip_grads.append(from_behind(d_input, "section", -(section_count - 1)))
        carried = d_input
    grads = (weight_grad.reshape(1, 3, 3, channels, channels), gain_grad[None], emb_grad[None])
    totals = lax.psum((grads[0], grads[1], grads[2]), ("dp", "space"))
    return (totals[0], totals[1], totals[2])


def solution(mesh):
    in_specs = (
        P("dp", "space", None, None),
        P("dp"),
        P("dp", "space", None, None),
        P("section", None, None, None, None),
        P("section", None),
        P("section", None, None),
    )
    out_specs = (P("section", None, None, None, None), P("section", None), P("section", None, None))
    return jax.shard_map(
        per_device, mesh=mesh, in_specs=in_specs, out_specs=out_specs, check_vma=False
    )
```

profile of v0, /device:TPU:32, one launch (start us, length us, event | category | flops | bytes accessed | tf_op | source)
XLA Modules:
  0.0 1326.5 jit_solution(16995887459301476496)
XLA Ops:
  9.3 3.0 collective-permute-start.16
  14.3 7.7 all-reduce.19
  24.2 1.3 collective-permute-start.1
  25.5 3.0 collective-permute-start
  28.6 1.4 constant_dynamic-update-slice_fusion.72
  30.6 1.6 copy.9
  34.2 10.0 collective-permute-start.9
  52.3 6.5 all-reduce.18
  59.2 1.3 collective-permute-start.4
  60.5 3.0 collective-permute-start.3
  65.0 1.6 collective-permute-start.13
  67.9 1.5 collective-permute-done.5
  70.5 7.2 all-reduce.17
  78.1 1.3 collective-permute-start.7
  79.4 3.0 collective-permute-start.6
  83.8 5.1 collective-permute-start.8
  89.0 1.5 collective-permute-done.8
  91.6 7.8 all-reduce.16
  100.3 1.3 collective-permute-start.11
  101.6 3.0 collective-permute-start.10
  106.8 5.8 collective-permute-start.12
  115.2 7.8 all-reduce.15
  124.7 1.4 fusion.60
  126.5 7.2 all-reduce.14
  134.1 1.3 collective-permute-start.18
  135.5 7.2 collective-permute-done.18
  142.6 1.3 collective-permute-start.20
  143.9 3.0 collective-permute-start.19
  147.0 1.3 collective-permute-start.25
  149.7 6.1 all-reduce.13
  156.1 1.3 collective-permute-start.21
  157.4 6.3 collective-permute-done.21
  165.1 3.0 collective-permute-start.22
  170.0 1.3 collective-permute-start.29
  172.4 7.5 all-reduce.12
  180.3 1.3 collective-permute-start.24
  181.7 6.2 collective-permute-done.24
  187.9 1.3 collective-permute-start.27
  189.2 3.0 collective-permute-start.26
  194.1 6.9 all-reduce.11
  201.4 1.3 collective-permute-start.15
  202.7 3.0 collective-permute-start.14
  207.1 6.6 collective-permute-done.28
  215.0 3.6 collective-permute-start.30
  221.6 1.9 convolution_add_fusion
  225.3 279.0 %psum.178 = f32[1,256]{1,0:T(1,128)} all-reduce(f32[1,256]{1,0:T(1,128)S(1)} %bitcast.511), channel_id=1, replica_groups=mesh['dp'=32,'section'=4,'space'=4] {'dp','space'}, use_global_device_ids=true, to_apply=%region_60.61 | all-reduce | flops 256 | bytes 2048 | tf_op jit(solution)/shard_map/psum | solution.py:223
  504.3 811.3 %all-reduce.22.cloned.1.call-done = (f32[1,3,3,256,256]{4,3,2,1,0:T(8,128)}, f32[1,256,512]{2,1,0:T(8,128)}) async-done(((f32[1,3,3,256,256]{4,3,2,1,0:T(8,128)}, f32[1,256,512]{2,1,0:T(8,128)}), (f32[1,3,3,256,256]{4,3,2,1,0:T(8,128)}, f32[1,256,512]{2,1,0:T(8,128)})) %all-reduce.22.cloned.1.call-update) | async-done | bytes 2883600 | tf_op jit(solution)/shard_map/psum | solution.py:223
  1315.6 3.3 copy.140
  (400 shorter events, 47.6 us)
Async XLA Ops:
  7.2 15.3 %copy-start = (bf16[1,256,512]{2,1,0:T(8,128)(2,1)S(1)}, bf16[1,256,512]{2,1,0:T(8,128)(2,1)}, u32[]{:S(2)}) copy-start(bf16[1,256,512]{2,1,0:T(8,128)(2,1)} %param.11) | copy-start | bytes 786436
  7.2 1308.4 %all-reduce.22.cloned.1.call-start = ((), (), s32[]{:S(2)}) async-start(), calls=%async_computation | async-start | bytes 5767168 | tf_op jit(solution)/shard_map/psum | solution.py:223
  8.0 37.5 %collective-permute-start.17 = (bf16[1,1,64,256]{3,2,1,0:T(8,128)(2,1)S(1)}, bf16[1,1,64,256]{3,2,1,0:T(8,128)(2,1)S(1)}, u32[]{:S(2)}, u32[]{:S(2)}) collective-permute-start(bf16[1,1,64,256]{3,2,1,0:T(8,128)(2,1)S(1)} %select_select_fusion.2), channel_id=1, source_target_pairs={{1,0},{2,1},{3,2},{5,4},{6,5},{7,6},{9,8},{10,9},{11,10},{13,12},{... | collective-permute-start | bytes 98312 | tf_op jit(solution)/shard_map/ppermute | solution.py:27
  9.3 36.3 %collective-permute-start.16 = (bf16[1,1,64,256]{3,2,1,0:T(8,128)(2,1)S(1)}, bf16[1,1,64,256]{3,2,1,0:T(8,128)(2,1)S(1)}, u32[]{:S(2)}, u32[]{:S(2)}) collective-permute-start(bf16[1,1,64,256]{3,2,1,0:T(8,128)(2,1)S(1)} %select_select_fusion.2), channel_id=1, source_target_pairs={{0,1},{1,2},{2,3},{4,5},{5,6},{6,7},{8,9},{9,10},{10,11},{12,13},{... | collective-permute-start | bytes 98312 | tf_op jit(solution)/shard_map/ppermute | solution.py:26
  24.2 9.0 collective-permute-start.1
  25.5 7.7 collective-permute-start
  33.4 14.7 %copy-start.5 = (bf16[2,1,64,256]{3,2,1,0:T(8,128)(2,1)S(1)}, bf16[2,1,64,256]{3,2,1,0:T(8,128)(2,1)}, u32[]{:S(2)}) copy-start(bf16[2,1,64,256]{3,2,1,0:T(8,128)(2,1)} %param.8) | copy-start | bytes 196612
  34.2 54.7 %collective-permute-start.9 = (bf16[1,1,64,256]{3,2,1,0:T(8,128)(2,1)S(1)}, bf16[1,1,64,256]{3,2,1,0:T(8,128)(2,1)S(1)}, u32[]{:S(2)}, u32[]{:S(2)}) collective-permute-start(bf16[1,1,64,256]{3,2,1,0:T(8,128)(2,1)S(1)} %fusion.8), channel_id=1, source_target_pairs={{0,12},{1,13},{2,14},{3,15},{16,28},{17,29},{18,30},{19,31},{32,44... | collective-permute-start | bytes 98312 | tf_op jit(solution)/shard_map/ppermute | solution.py:16
  44.3 7.0 collective-permute-start.2
  59.2 4.4 collective-permute-start.4
  60.5 3.9 collective-permute-start.3
  65.0 48.1 %collective-permute-start.13 = (bf16[1,1,64,256]{3,2,1,0:T(8,128)(2,1)S(1)}, bf16[1,1,64,256]{3,2,1,0:T(8,128)(2,1)S(1)}, u32[]{:S(2)}, u32[]{:S(2)}) collective-permute-start(bf16[1,1,64,256]{3,2,1,0:T(8,128)(2,1)S(1)} %fusion.6), channel_id=1, source_target_pairs={{0,12},{1,13},{2,14},{3,15},{16,28},{17,29},{18,30},{19,31},{32,44... | collective-permute-start | bytes 98312 | tf_op jit(solution)/shard_map/ppermute | solution.py:16
  66.6 2.9 collective-permute-start.5
  78.1 4.4 collective-permute-start.7
  79.4 3.9 collective-permute-start.6
  83.8 6.7 collective-permute-start.8
  100.3 12.3 copy-start.27
  100.3 4.4 collective-permute-start.11
  101.6 3.9 collective-permute-start.10
  105.6 19.1 %copy-start.3 = (bf16[3,3,256,256]{2,3,1,0:T(8,128)(2,1)S(1)}, bf16[3,3,256,256]{2,3,1,0:T(8,128)(2,1)}, u32[]{:S(2)}) copy-start(bf16[3,3,256,256]{2,3,1,0:T(8,128)(2,1)} %rev.3) | copy-start | bytes 3538948
  106.8 27.3 %copy-start.19 = (f32[1,256]{1,0:T(1,128)S(1)}, f32[1,256]{1,0:T(1,128)}, u32[]{:S(2)}) copy-start(f32[1,256]{1,0:T(1,128)} %get-tuple-element.96) | copy-start | bytes 3076
  106.8 7.3 collective-permute-start.12
  114.8 19.3 %copy-start.7 = (bf16[5,1,1,64,256]{4,3,2,1,0:T(8,128)(2,1)S(1)}, bf16[5,1,1,64,256]{4,3,2,1,0:T(8,128)(2,1)}, u32[]{:S(2)}) copy-start(bf16[5,1,1,64,256]{4,3,2,1,0:T(8,128)(2,1)} %get-tuple-element.70) | copy-start | bytes 491524
  124.6 24.2 %copy-start.18 = (f32[1,256]{1,0:T(1,128)S(1)}, f32[1,256]{1,0:T(1,128)}, u32[]{:S(2)}) copy-start(f32[1,256]{1,0:T(1,128)} %get-tuple-element.95) | copy-start | bytes 3076
  124.6 24.2 %copy-start.25 = (f32[1,256]{1,0:T(1,128)S(1)}, f32[1,256]{1,0:T(1,128)}, u32[]{:S(2)}) copy-start(f32[1,256]{1,0:T(1,128)} %get-tuple-element.105) | copy-start | bytes 3076
  134.1 8.5 collective-permute-start.18
  142.6 6.0 collective-permute-start.20
  143.9 4.7 collective-permute-start.19
  147.0 34.7 %collective-permute-start.25 = (bf16[1,1,64,256]{3,2,1,0:T(8,128)(2,1)S(1)}, bf16[1,1,64,256]{3,2,1,0:T(8,128)(2,1)S(1)}, u32[]{:S(2)}, u32[]{:S(2)}) collective-permute-start(bf16[1,1,64,256]{3,2,1,0:T(8,128)(2,1)S(1)} %fusion.123), channel_id=1, source_target_pairs={{12,0},{13,1},{14,2},{15,3},{28,16},{29,17},{30,18},{31,19},{44,32... | collective-permute-start | bytes 98312 | tf_op jit(solution)/shard_map/ppermute | solution.py:16
  148.8 22.7 %copy-start.17 = (f32[1,256]{1,0:T(1,128)S(1)}, f32[1,256]{1,0:T(1,128)}, u32[]{:S(2)}) copy-start(f32[1,256]{1,0:T(1,128)} %get-tuple-element.94) | copy-start | bytes 3076
  148.8 22.7 %copy-start.24 = (f32[1,256]{1,0:T(1,128)S(1)}, f32[1,256]{1,0:T(1,128)}, u32[]{:S(2)}) copy-start(f32[1,256]{1,0:T(1,128)} %get-tuple-element.104) | copy-start | bytes 3076
  156.1 7.6 collective-permute-start.21
  163.8 7.6 collective-permute-start.23
  165.1 6.3 collective-permute-start.22
  170.0 37.1 %collective-permute-start.29 = (bf16[1,1,64,256]{3,2,1,0:T(8,128)(2,1)S(1)}, bf16[1,1,64,256]{3,2,1,0:T(8,128)(2,1)S(1)}, u32[]{:S(2)}, u32[]{:S(2)}) collective-permute-start(bf16[1,1,64,256]{3,2,1,0:T(8,128)(2,1)S(1)} %fusion.75), channel_id=1, source_target_pairs={{12,0},{13,1},{14,2},{15,3},{28,16},{29,17},{30,18},{31,19},{44,32... | collective-permute-start | bytes 98312 | tf_op jit(solution)/shard_map/ppermute | solution.py:16
  171.6 21.7 %copy-start.14 = (f32[1,256]{1,0:T(1,128)S(1)}, f32[1,256]{1,0:T(1,128)}, u32[]{:S(2)}) copy-start(f32[1,256]{1,0:T(1,128)} %get-tuple-element.93) | copy-start | bytes 3076
  171.6 21.7 %copy-start.23 = (f32[1,256]{1,0:T(1,128)S(1)}, f32[1,256]{1,0:T(1,128)}, u32[]{:S(2)}) copy-start(f32[1,256]{1,0:T(1,128)} %get-tuple-element.103) | copy-start | bytes 3076
  180.3 7.5 collective-permute-start.24
  187.9 4.4 collective-permute-start.27
  189.2 3.9 collective-permute-start.26
  193.1 8.2 copy-start.15
  193.1 8.2 copy-start.16
  201.4 17.2 %collective-permute-start.15 = (bf16[1,1,64,256]{3,2,1,0:T(8,128)(2,1)S(1)}, bf16[1,1,64,256]{3,2,1,0:T(8,128)(2,1)S(1)}, u32[]{:S(2)}, u32[]{:S(2)}) collective-permute-start(bf16[1,1,64,256]{3,2,1,0:T(8,128)(2,1)S(1)} %get-tuple-element.118), channel_id=1, source_target_pairs={{1,0},{2,1},{3,2},{5,4},{6,5},{7,6},{9,8},{10,9},{11,10},{13,12},{... | collective-permute-start | bytes 98312 | tf_op jit(solution)/shard_map/ppermute | solution.py:27
  202.7 15.9 %collective-permute-start.14 = (bf16[1,1,64,256]{3,2,1,0:T(8,128)(2,1)S(1)}, bf16[1,1,64,256]{3,2,1,0:T(8,128)(2,1)S(1)}, u32[]{:S(2)}, u32[]{:S(2)}) collective-permute-start(bf16[1,1,64,256]{3,2,1,0:T(8,128)(2,1)S(1)} %get-tuple-element.118), channel_id=1, source_target_pairs={{0,1},{1,2},{2,3},{4,5},{5,6},{6,7},{8,9},{9,10},{10,11},{12,13},{... | collective-permute-start | bytes 98312 | tf_op jit(solution)/shard_map/ppermute | solution.py:26
  205.8 7.9 collective-permute-start.28
  213.7 9.8 collective-permute-start.31
  215.0 8.5 collective-permute-start.30
  1315.6 3.3 copy-start.4
  (13 other events, 14.1 us)
Sparse Core Ops, SparseCore 0:
  225.4 1090.1 all-reduce.21
where the time goes:
time: 1330 us
  waiting for transfers between devices  845 us (64%)
  blocking collectives  344 us (26%)
  starting transfers between devices  76.6 us (6%)
  local copies, waits for them, and re-layouts  20.9 us (2%)
  between operations  16.3 us (1%)
  other arithmetic  15.7 us (1%)
    psum x1, waiting for transfers between devices, per_device(): totals = lax.psum((grads[0], grads[1], grads[2]), ('dp', 'space'))  811 us
    psum x1, blocking collectives, per_device(): totals = lax.psum((grads[0], grads[1], grads[2]), ('dp', 'space'))  279 us
    psum x5, blocking collectives, per_device(): first_sum, square_sum = lax.psum((first_sum, square_sum), 'space')  36.9 us
    ppermute x12, starting transfers between devices, from_behind(): lax.ppermute(value, axis, [(source, source + steps) for source in range(i...  32.8 us
    ppermute x10, starting transfers between devices, extended(): before = lax.ppermute(last, axis, up)  30.9 us
    ppermute x12, waiting for transfers between devices, from_behind(): lax.ppermute(value, axis, [(source, source + steps) for source in range(i...  30.4 us
    psum x4, blocking collectives, per_device(): d_first, d_square = lax.psum((d_first, d_square), 'space')  27.7 us
  transfers between devices with their start and end apart: 33, of which 12 were waited for; matrix products, arithmetic and copies ran while one was open for 2% of the time, Pallas kernels for 0%

commit v1 on v0

--- a/solution.py
+++ b/solution.py
@@ -220,7 +220,8 @@
             skip_grads.append(from_behind(d_input, "section", -(section_count - 1)))
         carried = d_input
     grads = (weight_grad.reshape(1, 3, 3, channels, channels), gain_grad[None], emb_grad[None])
-    totals = lax.psum((grads[0], grads[1], grads[2]), ("dp", "space"))
+    half = lax.psum((grads[0], grads[1], grads[2]), "space")
+    totals = lax.psum(half, "dp")
     return (totals[0], totals[1], totals[2])
 
 

time: 1330 us -> 491 us (0.37)
  the two profiles are of different devices: /device:TPU:32 before, /device:TPU:64 now
where the time goes in v1:
time: 491 us; the launch traced here: 490 us
  waiting for transfers between devices  214 us (44%)
  blocking collectives  142 us (29%)
  starting transfers between devices  72.8 us (15%)
  local copies, waits for them, and re-layouts  20.9 us (4%)
  between operations  16.3 us (3%)
  other arithmetic  15.7 us (3%)
  matrix products  8.33 us (2%)
    psum x1, waiting for transfers between devices, per_device(): totals = lax.psum(half, 'dp')  91.5 us
    psum x1, waiting for transfers between devices, per_device(): half = lax.psum((grads[0], grads[1], grads[2]), 'space')  79.8 us
    psum x1, blocking collectives, per_device(): totals = lax.psum(half, 'dp')  75.2 us
    psum x5, blocking collectives, per_device(): first_sum, square_sum = lax.psum((first_sum, square_sum), 'space')  34.3 us
    ppermute x12, waiting for transfers between devices, from_behind(): lax.ppermute(value, axis, [(source, source + steps) for source in range(i...  30.4 us
    ppermute x12, starting transfers between devices, from_behind(): lax.ppermute(value, axis, [(source, source + steps) for source in range(i...  29.3 us
    psum x4, blocking collectives, per_device(): d_first, d_square = lax.psum((d_first, d_square), 'space')  24.5 us
    ppermute x10, starting transfers between devices, extended(): before = lax.ppermute(last, axis, up)  23.8 us
  transfers between devices with their start and end apart: 34, of which 14 were waited for; matrix products, arithmetic and copies ran while one was open for 7% of the time, Pallas kernels for 0%

profile of v1, /device:TPU:64, one launch (start us, length us, event | category | flops | bytes accessed | tf_op | source)
XLA Modules:
  0.0 490.0 jit_solution(10379304335655059604)
XLA Ops:
  8.0 1.9 collective-permute-start.17
  9.9 2.4 collective-permute-start.16
  14.3 10.4 %all-reduce.19 = (f32[1,32]{1,0:T(1,128)S(1)}, f32[1,32]{1,0:T(1,128)S(1)}) all-reduce(f32[1,32]{1,0:T(1,128)S(1)} %bitcast.533, f32[1,32]{1,0:T(1,128)S(1)} %bitcast.532), channel_id=1, replica_groups=mesh['dp'=32,'section'=4,'space'=4] {'space'}, use_global_device_ids=true, to_apply=%region_5.6 | all-reduce | flops 64 | bytes 512 | tf_op jit(solution)/shard_map/psum | solution.py:145
  26.9 1.9 collective-permute-start.1
  28.8 2.4 collective-permute-start
  33.2 1.6 copy.9
  36.9 6.5 %collective-permute-start.9 = (bf16[1,1,64,256]{3,2,1,0:T(8,128)(2,1)S(1)}, bf16[1,1,64,256]{3,2,1,0:T(8,128)(2,1)S(1)}, u32[]{:S(2)}, u32[]{:S(2)}) collective-permute-start(bf16[1,1,64,256]{3,2,1,0:T(8,128)(2,1)S(1)} %fusion.8), channel_id=1, source_target_pairs={{0,12},{1,13},{2,14},{3,15},{16,28},{17,29},{18,30},{19,31},{32,44... | collective-permute-start | bytes 98312 | tf_op jit(solution)/shard_map/ppermute | solution.py:16
  51.5 6.6 %all-reduce.18 = (f32[1,32]{1,0:T(1,128)S(1)}, f32[1,32]{1,0:T(1,128)S(1)}) all-reduce(f32[1,32]{1,0:T(1,128)S(1)} %bitcast.534, f32[1,32]{1,0:T(1,128)S(1)} %bitcast.528), channel_id=1, replica_groups=mesh['dp'=32,'section'=4,'space'=4] {'space'}, use_global_device_ids=true, to_apply=%region_11.12 | all-reduce | flops 64 | bytes 512 | tf_op jit(solution)/shard_map/psum | solution.py:145
  58.5 1.9 collective-permute-start.4
  60.4 2.4 collective-permute-start.3
  62.9 2.8 collective-permute-done.3
  66.2 1.6 collective-permute-start.13
  71.7 5.8 %all-reduce.17 = (f32[1,32]{1,0:T(1,128)S(1)}, f32[1,32]{1,0:T(1,128)S(1)}) all-reduce(f32[1,32]{1,0:T(1,128)S(1)} %bitcast.535, f32[1,32]{1,0:T(1,128)S(1)} %bitcast.529), channel_id=1, replica_groups=mesh['dp'=32,'section'=4,'space'=4] {'space'}, use_global_device_ids=true, to_apply=%region_17.18 | all-reduce | flops 64 | bytes 512 | tf_op jit(solution)/shard_map/psum | solution.py:145
  77.9 1.9 collective-permute-start.7
  79.8 2.4 collective-permute-start.6
  82.3 2.8 collective-permute-done.6
  85.6 5.1 %collective-permute-start.8 = (bf16[1,1,64,256]{3,2,1,0:T(8,128)(2,1)S(1)}, bf16[1,1,64,256]{3,2,1,0:T(8,128)(2,1)S(1)}, u32[]{:S(2)}, u32[]{:S(2)}) collective-permute-start(bf16[1,1,64,256]{3,2,1,0:T(8,128)(2,1)S(1)} %fusion.5), channel_id=1, source_target_pairs={{0,4},{4,8},{8,12},{1,5},{5,9},{9,13},{2,6},{6,10},{10,14},{3,7},{... | collective-permute-start | bytes 98312 | tf_op jit(solution)/shard_map/ppermute | solution.py:16
  93.4 5.8 %all-reduce.16 = (f32[1,32]{1,0:T(1,128)S(1)}, f32[1,32]{1,0:T(1,128)S(1)}) all-reduce(f32[1,32]{1,0:T(1,128)S(1)} %bitcast.536, f32[1,32]{1,0:T(1,128)S(1)} %bitcast.530), channel_id=1, replica_groups=mesh['dp'=32,'section'=4,'space'=4] {'space'}, use_global_device_ids=true, to_apply=%region_23.24 | all-reduce | flops 64 | bytes 512 | tf_op jit(solution)/shard_map/psum | solution.py:145
  100.1 1.9 collective-permute-start.11
  102.1 2.4 collective-permute-start.10
  104.5 2.8 collective-permute-done.10
  108.6 5.8 %collective-permute-start.12 = (bf16[1,1,64,256]{3,2,1,0:T(8,128)(2,1)S(1)}, bf16[1,1,64,256]{3,2,1,0:T(8,128)(2,1)S(1)}, u32[]{:S(2)}, u32[]{:S(2)}) collective-permute-start(bf16[1,1,64,256]{3,2,1,0:T(8,128)(2,1)S(1)} %fusion.4), channel_id=1, source_target_pairs={{0,4},{4,8},{8,12},{1,5},{5,9},{9,13},{2,6},{6,10},{10,14},{3,7},{... | collective-permute-start | bytes 98312 | tf_op jit(solution)/shard_map/ppermute | solution.py:16
  117.0 5.8 %all-reduce.15 = (f32[1,32]{1,0:T(1,128)S(1)}, f32[1,32]{1,0:T(1,128)S(1)}) all-reduce(f32[1,32]{1,0:T(1,128)S(1)} %bitcast.537, f32[1,32]{1,0:T(1,128)S(1)} %bitcast.531), channel_id=1, replica_groups=mesh['dp'=32,'section'=4,'space'=4] {'space'}, use_global_device_ids=true, to_apply=%region_29.30 | all-reduce | flops 64 | bytes 512 | tf_op jit(solution)/shard_map/psum | solution.py:145
  126.3 5.8 %all-reduce.14 = (f32[1,32]{1,0:T(1,128)S(1)}, f32[32]{0:T(128)S(1)}) all-reduce(f32[1,32]{1,0:T(1,128)S(1)} %broadcast_multiply_fusion.3, f32[32]{0:T(128)S(1)} %get-tuple-element.70), channel_id=1, replica_groups=mesh['dp'=32,'section'=4,'space'=4] {'space'}, use_global_device_ids=true, to_apply=%region_35.36 | all-reduce | flops 64 | bytes 512 | tf_op jit(solution)/shard_map/psum | solution.py:210
  133.8 6.9 %collective-permute-done.18 = bf16[1,1,64,256]{3,2,1,0:T(8,128)(2,1)S(1)} collective-permute-done((bf16[1,1,64,256]{3,2,1,0:T(8,128)(2,1)S(1)}, bf16[1,1,64,256]{3,2,1,0:T(8,128)(2,1)S(1)}, u32[]{:S(2)}, u32[]{:S(2)}) %collective-permute-start.18) | collective-permute-done | bytes 32800 | tf_op jit(solution)/shard_map/ppermute | solution.py:16
  140.8 1.9 collective-permute-start.20
  142.7 2.4 collective-permute-start.19
  149.0 6.0 %all-reduce.13 = (f32[1,32]{1,0:T(1,128)S(1)}, f32[32]{0:T(128)S(1)}) all-reduce(f32[1,32]{1,0:T(1,128)S(1)} %broadcast_multiply_fusion.2, f32[32]{0:T(128)S(1)} %get-tuple-element.66), channel_id=1, replica_groups=mesh['dp'=32,'section'=4,'space'=4] {'space'}, use_global_device_ids=true, to_apply=%region_41.42 | all-reduce | flops 64 | bytes 512 | tf_op jit(solution)/shard_map/psum | solution.py:210
  156.7 6.8 %collective-permute-done.21 = bf16[1,1,64,256]{3,2,1,0:T(8,128)(2,1)S(1)} collective-permute-done((bf16[1,1,64,256]{3,2,1,0:T(8,128)(2,1)S(1)}, bf16[1,1,64,256]{3,2,1,0:T(8,128)(2,1)S(1)}, u32[]{:S(2)}, u32[]{:S(2)}) %collective-permute-start.21) | collective-permute-done | bytes 32800 | tf_op jit(solution)/shard_map/ppermute | solution.py:16
  163.5 1.9 collective-permute-start.23
  165.5 2.4 collective-permute-start.22
  172.2 6.9 %all-reduce.12 = (f32[1,32]{1,0:T(1,128)S(1)}, f32[32]{0:T(128)S(1)}) all-reduce(f32[1,32]{1,0:T(1,128)S(1)} %broadcast_multiply_fusion.1, f32[32]{0:T(128)S(1)} %get-tuple-element.62), channel_id=1, replica_groups=mesh['dp'=32,'section'=4,'space'=4] {'space'}, use_global_device_ids=true, to_apply=%region_47.48 | all-reduce | flops 64 | bytes 512 | tf_op jit(solution)/shard_map/psum | solution.py:210
  180.8 6.0 %collective-permute-done.24 = bf16[1,1,64,256]{3,2,1,0:T(8,128)(2,1)S(1)} collective-permute-done((bf16[1,1,64,256]{3,2,1,0:T(8,128)(2,1)S(1)}, bf16[1,1,64,256]{3,2,1,0:T(8,128)(2,1)S(1)}, u32[]{:S(2)}, u32[]{:S(2)}) %collective-permute-start.24) | collective-permute-done | bytes 32800 | tf_op jit(solution)/shard_map/ppermute | solution.py:16
  186.8 1.9 collective-permute-start.27
  188.7 2.4 collective-permute-start.26
  191.2 2.8 collective-permute-done.26
  195.0 5.8 %all-reduce.11 = (f32[1,32]{1,0:T(1,128)S(1)}, f32[32]{0:T(128)S(1)}) all-reduce(f32[1,32]{1,0:T(1,128)S(1)} %broadcast_multiply_fusion, f32[32]{0:T(128)S(1)} %get-tuple-element.58), channel_id=1, replica_groups=mesh['dp'=32,'section'=4,'space'=4] {'space'}, use_global_device_ids=true, to_apply=%region_53.54 | all-reduce | flops 64 | bytes 512 | tf_op jit(solution)/shard_map/psum | solution.py:210
  201.2 1.9 collective-permute-start.15
  203.1 2.4 collective-permute-start.14
  206.9 6.6 %collective-permute-done.28 = bf16[1,1,64,256]{3,2,1,0:T(8,128)(2,1)S(1)} collective-permute-done((bf16[1,1,64,256]{3,2,1,0:T(8,128)(2,1)S(1)}, bf16[1,1,64,256]{3,2,1,0:T(8,128)(2,1)S(1)}, u32[]{:S(2)}, u32[]{:S(2)}) %collective-permute-start.28) | collective-permute-done | bytes 32800 | tf_op jit(solution)/shard_map/ppermute | solution.py:16
  213.5 2.3 collective-permute-start.31
  215.8 2.2 collective-permute-start.30
  221.0 1.9 convolution_add_fusion
  224.7 79.8 %all-reduce.26.cloned.1.call-done = (f32[1,3,3,256,256]{4,3,2,1,0:T(8,128)}, f32[1,256,512]{2,1,0:T(8,128)}) async-done(((f32[1,3,3,256,256]{4,3,2,1,0:T(8,128)}, f32[1,256,512]{2,1,0:T(8,128)}), (f32[1,3,3,256,256]{4,3,2,1,0:T(8,128)}, f32[1,256,512]{2,1,0:T(8,128)})) %all-reduce.26.cloned.1.call-update) | async-done | bytes 2883600 | tf_op jit(solution)/shard_map/psum | solution.py:223
  304.6 7.8 %psum.200 = f32[1,256]{1,0:T(1,128)S(1)} all-reduce(f32[1,256]{1,0:T(1,128)S(1)} %bitcast.511), channel_id=1, replica_groups=mesh['dp'=32,'section'=4,'space'=4] {'space'}, use_global_device_ids=true, to_apply=%region_61.62 | all-reduce | flops 256 | bytes 2048 | tf_op jit(solution)/shard_map/psum | solution.py:223
  312.3 75.2 %psum.201 = f32[1,256]{1,0:T(1,128)} all-reduce(f32[1,256]{1,0:T(1,128)S(1)} %psum.200), channel_id=1, replica_groups=mesh['dp'=32,'section'=4,'space'=4] {'dp'}, use_global_device_ids=true, to_apply=%region_62.63 | all-reduce | flops 256 | bytes 2048 | tf_op jit(solution)/shard_map/psum | solution.py:224
  387.6 91.5 %all-reduce.24.cloned.1.call-done = (f32[1,3,3,256,256]{4,3,2,1,0:T(8,128)}, f32[1,256,512]{2,1,0:T(8,128)}) async-done(((f32[1,3,3,256,256]{4,3,2,1,0:T(8,128)}, f32[1,256,512]{2,1,0:T(8,128)}), (f32[1,3,3,256,256]{4,3,2,1,0:T(8,128)}, f32[1,256,512]{2,1,0:T(8,128)})) %all-reduce.24.cloned.1.call-update) | async-done | bytes 2883600 | tf_op jit(solution)/shard_map/psum | solution.py:224
  479.1 3.3 copy.142
  (404 shorter events, 54.0 us)
Async XLA Ops:
  7.2 18.0 %copy-start = (bf16[1,256,512]{2,1,0:T(8,128)(2,1)S(1)}, bf16[1,256,512]{2,1,0:T(8,128)(2,1)}, u32[]{:S(2)}) copy-start(bf16[1,256,512]{2,1,0:T(8,128)(2,1)} %param.11) | copy-start | bytes 786436
  7.2 297.3 %all-reduce.26.cloned.1.call-start = ((), (), s32[]{:S(2)}) async-start(), calls=%async_computation.1 | async-start | bytes 5767168 | tf_op jit(solution)/shard_map/psum | solution.py:223
  8.0 36.7 %collective-permute-start.17 = (bf16[1,1,64,256]{3,2,1,0:T(8,128)(2,1)S(1)}, bf16[1,1,64,256]{3,2,1,0:T(8,128)(2,1)S(1)}, u32[]{:S(2)}, u32[]{:S(2)}) collective-permute-start(bf16[1,1,64,256]{3,2,1,0:T(8,128)(2,1)S(1)} %select_select_fusion.2), channel_id=1, source_target_pairs={{1,0},{2,1},{3,2},{5,4},{6,5},{7,6},{9,8},{10,9},{11,10},{13,12},{... | collective-permute-start | bytes 98312 | tf_op jit(solution)/shard_map/ppermute | solution.py:27
  9.9 34.8 %collective-permute-start.16 = (bf16[1,1,64,256]{3,2,1,0:T(8,128)(2,1)S(1)}, bf16[1,1,64,256]{3,2,1,0:T(8,128)(2,1)S(1)}, u32[]{:S(2)}, u32[]{:S(2)}) collective-permute-start(bf16[1,1,64,256]{3,2,1,0:T(8,128)(2,1)S(1)} %select_select_fusion.2), channel_id=1, source_target_pairs={{0,1},{1,2},{2,3},{4,5},{5,6},{6,7},{8,9},{9,10},{10,11},{12,13},{... | collective-permute-start | bytes 98312 | tf_op jit(solution)/shard_map/ppermute | solution.py:26
  26.9 9.0 %collective-permute-start.1 = (bf16[1,1,64,256]{3,2,1,0:T(8,128)(2,1)S(1)}, bf16[1,1,64,256]{3,2,1,0:T(8,128)(2,1)S(1)}, u32[]{:S(2)}, u32[]{:S(2)}) collective-permute-start(bf16[1,1,64,256]{3,2,1,0:T(8,128)(2,1)S(1)} %multiply_convert_fusion.4), channel_id=1, source_target_pairs={{1,0},{2,1},{3,2},{5,4},{6,5},{7,6},{9,8},{10,9},{11,10},{13,12},{... | collective-permute-start | bytes 98312 | tf_op jit(solution)/shard_map/ppermute | solution.py:27
  28.8 7.1 %collective-permute-start = (bf16[1,1,64,256]{3,2,1,0:T(8,128)(2,1)S(1)}, bf16[1,1,64,256]{3,2,1,0:T(8,128)(2,1)S(1)}, u32[]{:S(2)}, u32[]{:S(2)}) collective-permute-start(bf16[1,1,64,256]{3,2,1,0:T(8,128)(2,1)S(1)} %multiply_convert_fusion.4), channel_id=1, source_target_pairs={{0,1},{1,2},{2,3},{4,5},{5,6},{6,7},{8,9},{9,10},{10,11},{12,13},{... | collective-permute-start | bytes 98312 | tf_op jit(solution)/shard_map/ppermute | solution.py:26
  36.0 11.2 %copy-start.5 = (bf16[2,1,64,256]{3,2,1,0:T(8,128)(2,1)S(1)}, bf16[2,1,64,256]{3,2,1,0:T(8,128)(2,1)}, u32[]{:S(2)}) copy-start(bf16[2,1,64,256]{3,2,1,0:T(8,128)(2,1)} %param.8) | copy-start | bytes 196612
  36.9 53.9 %collective-permute-start.9 = (bf16[1,1,64,256]{3,2,1,0:T(8,128)(2,1)S(1)}, bf16[1,1,64,256]{3,2,1,0:T(8,128)(2,1)S(1)}, u32[]{:S(2)}, u32[]{:S(2)}) collective-permute-start(bf16[1,1,64,256]{3,2,1,0:T(8,128)(2,1)S(1)} %fusion.8), channel_id=1, source_target_pairs={{0,12},{1,13},{2,14},{3,15},{16,28},{17,29},{18,30},{19,31},{32,44... | collective-permute-start | bytes 98312 | tf_op jit(solution)/shard_map/ppermute | solution.py:16
  43.4 7.0 %collective-permute-start.2 = (bf16[1,1,64,256]{3,2,1,0:T(8,128)(2,1)S(1)}, bf16[1,1,64,256]{3,2,1,0:T(8,128)(2,1)S(1)}, u32[]{:S(2)}, u32[]{:S(2)}) collective-permute-start(bf16[1,1,64,256]{3,2,1,0:T(8,128)(2,1)S(1)} %fusion.8), channel_id=1, source_target_pairs={{0,4},{4,8},{8,12},{1,5},{5,9},{9,13},{2,6},{6,10},{10,14},{3,7},{... | collective-permute-start | bytes 98312 | tf_op jit(solution)/shard_map/ppermute | solution.py:16
  58.5 4.4 collective-permute-start.4
  60.4 5.2 %collective-permute-start.3 = (bf16[1,1,64,256]{3,2,1,0:T(8,128)(2,1)S(1)}, bf16[1,1,64,256]{3,2,1,0:T(8,128)(2,1)S(1)}, u32[]{:S(2)}, u32[]{:S(2)}) collective-permute-start(bf16[1,1,64,256]{3,2,1,0:T(8,128)(2,1)S(1)} %multiply_convert_fusion.3), channel_id=1, source_target_pairs={{0,1},{1,2},{2,3},{4,5},{5,6},{6,7},{8,9},{9,10},{10,11},{12,13},{... | collective-permute-start | bytes 98312 | tf_op jit(solution)/shard_map/ppermute | solution.py:26
  66.2 48.7 %collective-permute-start.13 = (bf16[1,1,64,256]{3,2,1,0:T(8,128)(2,1)S(1)}, bf16[1,1,64,256]{3,2,1,0:T(8,128)(2,1)S(1)}, u32[]{:S(2)}, u32[]{:S(2)}) collective-permute-start(bf16[1,1,64,256]{3,2,1,0:T(8,128)(2,1)S(1)} %fusion.6), channel_id=1, source_target_pairs={{0,12},{1,13},{2,14},{3,15},{16,28},{17,29},{18,30},{19,31},{32,44... | collective-permute-start | bytes 98312 | tf_op jit(solution)/shard_map/ppermute | solution.py:16
  67.8 2.9 collective-permute-start.5
  77.9 4.4 collective-permute-start.7
  79.8 5.2 %collective-permute-start.6 = (bf16[1,1,64,256]{3,2,1,0:T(8,128)(2,1)S(1)}, bf16[1,1,64,256]{3,2,1,0:T(8,128)(2,1)S(1)}, u32[]{:S(2)}, u32[]{:S(2)}) collective-permute-start(bf16[1,1,64,256]{3,2,1,0:T(8,128)(2,1)S(1)} %multiply_convert_fusion.2), channel_id=1, source_target_pairs={{0,1},{1,2},{2,3},{4,5},{5,6},{6,7},{8,9},{9,10},{10,11},{12,13},{... | collective-permute-start | bytes 98312 | tf_op jit(solution)/shard_map/ppermute | solution.py:26
  85.6 6.7 %collective-permute-start.8 = (bf16[1,1,64,256]{3,2,1,0:T(8,128)(2,1)S(1)}, bf16[1,1,64,256]{3,2,1,0:T(8,128)(2,1)S(1)}, u32[]{:S(2)}, u32[]{:S(2)}) collective-permute-start(bf16[1,1,64,256]{3,2,1,0:T(8,128)(2,1)S(1)} %fusion.5), channel_id=1, source_target_pairs={{0,4},{4,8},{8,12},{1,5},{5,9},{9,13},{2,6},{6,10},{10,14},{3,7},{... | collective-permute-start | bytes 98312 | tf_op jit(solution)/shard_map/ppermute | solution.py:16
  100.1 14.3 %copy-start.27 = (f32[1,32]{1,0:T(1,128)S(1)}, f32[1,32]{1,0:T(1,128)}, u32[]{:S(2)}) copy-start(f32[1,32]{1,0:T(1,128)} %copy-done.26) | copy-start | bytes 388
  100.1 4.4 collective-permute-start.11
  102.1 5.2 %collective-permute-start.10 = (bf16[1,1,64,256]{3,2,1,0:T(8,128)(2,1)S(1)}, bf16[1,1,64,256]{3,2,1,0:T(8,128)(2,1)S(1)}, u32[]{:S(2)}, u32[]{:S(2)}) collective-permute-start(bf16[1,1,64,256]{3,2,1,0:T(8,128)(2,1)S(1)} %multiply_convert_fusion.1), channel_id=1, source_target_pairs={{0,1},{1,2},{2,3},{4,5},{5,6},{6,7},{8,9},{9,10},{10,11},{12,13},{... | collective-permute-start | bytes 98312 | tf_op jit(solution)/shard_map/ppermute | solution.py:26
  107.4 17.1 %copy-start.3 = (bf16[3,3,256,256]{2,3,1,0:T(8,128)(2,1)S(1)}, bf16[3,3,256,256]{2,3,1,0:T(8,128)(2,1)}, u32[]{:S(2)}) copy-start(bf16[3,3,256,256]{2,3,1,0:T(8,128)(2,1)} %rev.3) | copy-start | bytes 3538948
  108.6 23.8 %copy-start.19 = (f32[1,256]{1,0:T(1,128)S(1)}, f32[1,256]{1,0:T(1,128)}, u32[]{:S(2)}) copy-start(f32[1,256]{1,0:T(1,128)} %get-tuple-element.98) | copy-start | bytes 3076
  108.6 7.3 %collective-permute-start.12 = (bf16[1,1,64,256]{3,2,1,0:T(8,128)(2,1)S(1)}, bf16[1,1,64,256]{3,2,1,0:T(8,128)(2,1)S(1)}, u32[]{:S(2)}, u32[]{:S(2)}) collective-permute-start(bf16[1,1,64,256]{3,2,1,0:T(8,128)(2,1)S(1)} %fusion.4), channel_id=1, source_target_pairs={{0,4},{4,8},{8,12},{1,5},{5,9},{9,13},{2,6},{6,10},{10,14},{3,7},{... | collective-permute-start | bytes 98312 | tf_op jit(solution)/shard_map/ppermute | solution.py:16
  116.6 15.9 %copy-start.7 = (bf16[5,1,1,64,256]{4,3,2,1,0:T(8,128)(2,1)S(1)}, bf16[5,1,1,64,256]{4,3,2,1,0:T(8,128)(2,1)}, u32[]{:S(2)}) copy-start(bf16[5,1,1,64,256]{4,3,2,1,0:T(8,128)(2,1)} %get-tuple-element.72) | copy-start | bytes 491524
  124.5 23.6 %copy-start.18 = (f32[1,256]{1,0:T(1,128)S(1)}, f32[1,256]{1,0:T(1,128)}, u32[]{:S(2)}) copy-start(f32[1,256]{1,0:T(1,128)} %get-tuple-element.97) | copy-start | bytes 3076
  124.5 23.6 %copy-start.25 = (f32[1,256]{1,0:T(1,128)S(1)}, f32[1,256]{1,0:T(1,128)}, u32[]{:S(2)}) copy-start(f32[1,256]{1,0:T(1,128)} %get-tuple-element.107) | copy-start | bytes 3076
  132.5 8.3 %collective-permute-start.18 = (bf16[1,1,64,256]{3,2,1,0:T(8,128)(2,1)S(1)}, bf16[1,1,64,256]{3,2,1,0:T(8,128)(2,1)S(1)}, u32[]{:S(2)}, u32[]{:S(2)}) collective-permute-start(bf16[1,1,64,256]{3,2,1,0:T(8,128)(2,1)S(1)} %fusion.123), channel_id=1, source_target_pairs={{4,0},{8,4},{12,8},{5,1},{9,5},{13,9},{6,2},{10,6},{14,10},{7,3},{... | collective-permute-start | bytes 98312 | tf_op jit(solution)/shard_map/ppermute | solution.py:16
  140.8 6.0 %collective-permute-start.20 = (bf16[1,1,64,256]{3,2,1,0:T(8,128)(2,1)S(1)}, bf16[1,1,64,256]{3,2,1,0:T(8,128)(2,1)S(1)}, u32[]{:S(2)}, u32[]{:S(2)}) collective-permute-start(bf16[1,1,64,256]{3,2,1,0:T(8,128)(2,1)S(1)} %select_select_fusion.1), channel_id=1, source_target_pairs={{1,0},{2,1},{3,2},{5,4},{6,5},{7,6},{9,8},{10,9},{11,10},{13,12},{... | collective-permute-start | bytes 98312 | tf_op jit(solution)/shard_map/ppermute | solution.py:27
  142.7 5.2 %collective-permute-start.19 = (bf16[1,1,64,256]{3,2,1,0:T(8,128)(2,1)S(1)}, bf16[1,1,64,256]{3,2,1,0:T(8,128)(2,1)S(1)}, u32[]{:S(2)}, u32[]{:S(2)}) collective-permute-start(bf16[1,1,64,256]{3,2,1,0:T(8,128)(2,1)S(1)} %select_select_fusion.1), channel_id=1, source_target_pairs={{0,1},{1,2},{2,3},{4,5},{5,6},{6,7},{8,9},{9,10},{10,11},{12,13},{... | collective-permute-start | bytes 98312 | tf_op jit(solution)/shard_map/ppermute | solution.py:26
  145.1 35.7 %collective-permute-start.25 = (bf16[1,1,64,256]{3,2,1,0:T(8,128)(2,1)S(1)}, bf16[1,1,64,256]{3,2,1,0:T(8,128)(2,1)S(1)}, u32[]{:S(2)}, u32[]{:S(2)}) collective-permute-start(bf16[1,1,64,256]{3,2,1,0:T(8,128)(2,1)S(1)} %fusion.123), channel_id=1, source_target_pairs={{12,0},{13,1},{14,2},{15,3},{28,16},{29,17},{30,18},{31,19},{44,32... | collective-permute-start | bytes 98312 | tf_op jit(solution)/shard_map/ppermute | solution.py:16
  148.1 23.2 %copy-start.17 = (f32[1,256]{1,0:T(1,128)S(1)}, f32[1,256]{1,0:T(1,128)}, u32[]{:S(2)}) copy-start(f32[1,256]{1,0:T(1,128)} %get-tuple-element.96) | copy-start | bytes 3076
  148.1 23.2 %copy-start.24 = (f32[1,256]{1,0:T(1,128)S(1)}, f32[1,256]{1,0:T(1,128)}, u32[]{:S(2)}) copy-start(f32[1,256]{1,0:T(1,128)} %get-tuple-element.106) | copy-start | bytes 3076
  155.4 8.1 %collective-permute-start.21 = (bf16[1,1,64,256]{3,2,1,0:T(8,128)(2,1)S(1)}, bf16[1,1,64,256]{3,2,1,0:T(8,128)(2,1)S(1)}, u32[]{:S(2)}, u32[]{:S(2)}) collective-permute-start(bf16[1,1,64,256]{3,2,1,0:T(8,128)(2,1)S(1)} %fusion.75), channel_id=1, source_target_pairs={{4,0},{8,4},{12,8},{5,1},{9,5},{13,9},{6,2},{10,6},{14,10},{7,3},{... | collective-permute-start | bytes 98312 | tf_op jit(solution)/shard_map/ppermute | solution.py:16
  163.5 7.6 %collective-permute-start.23 = (bf16[1,1,64,256]{3,2,1,0:T(8,128)(2,1)S(1)}, bf16[1,1,64,256]{3,2,1,0:T(8,128)(2,1)S(1)}, u32[]{:S(2)}, u32[]{:S(2)}) collective-permute-start(bf16[1,1,64,256]{3,2,1,0:T(8,128)(2,1)S(1)} %select_select_fusion), channel_id=1, source_target_pairs={{1,0},{2,1},{3,2},{5,4},{6,5},{7,6},{9,8},{10,9},{11,10},{13,12},{... | collective-permute-start | bytes 98312 | tf_op jit(solution)/shard_map/ppermute | solution.py:27
  165.5 5.7 %collective-permute-start.22 = (bf16[1,1,64,256]{3,2,1,0:T(8,128)(2,1)S(1)}, bf16[1,1,64,256]{3,2,1,0:T(8,128)(2,1)S(1)}, u32[]{:S(2)}, u32[]{:S(2)}) collective-permute-start(bf16[1,1,64,256]{3,2,1,0:T(8,128)(2,1)S(1)} %select_select_fusion), channel_id=1, source_target_pairs={{0,1},{1,2},{2,3},{4,5},{5,6},{6,7},{8,9},{9,10},{10,11},{12,13},{... | collective-permute-start | bytes 98312 | tf_op jit(solution)/shard_map/ppermute | solution.py:26
  169.8 37.1 %collective-permute-start.29 = (bf16[1,1,64,256]{3,2,1,0:T(8,128)(2,1)S(1)}, bf16[1,1,64,256]{3,2,1,0:T(8,128)(2,1)S(1)}, u32[]{:S(2)}, u32[]{:S(2)}) collective-permute-start(bf16[1,1,64,256]{3,2,1,0:T(8,128)(2,1)S(1)} %fusion.75), channel_id=1, source_target_pairs={{12,0},{13,1},{14,2},{15,3},{28,16},{29,17},{30,18},{31,19},{44,32... | collective-permute-start | bytes 98312 | tf_op jit(solution)/shard_map/ppermute | solution.py:16
  171.3 22.8 %copy-start.14 = (f32[1,256]{1,0:T(1,128)S(1)}, f32[1,256]{1,0:T(1,128)}, u32[]{:S(2)}) copy-start(f32[1,256]{1,0:T(1,128)} %get-tuple-element.95) | copy-start | bytes 3076
  171.4 22.8 %copy-start.23 = (f32[1,256]{1,0:T(1,128)S(1)}, f32[1,256]{1,0:T(1,128)}, u32[]{:S(2)}) copy-start(f32[1,256]{1,0:T(1,128)} %get-tuple-element.105) | copy-start | bytes 3076
  179.5 7.3 %collective-permute-start.24 = (bf16[1,1,64,256]{3,2,1,0:T(8,128)(2,1)S(1)}, bf16[1,1,64,256]{3,2,1,0:T(8,128)(2,1)S(1)}, u32[]{:S(2)}, u32[]{:S(2)}) collective-permute-start(bf16[1,1,64,256]{3,2,1,0:T(8,128)(2,1)S(1)} %fusion.79), channel_id=1, source_target_pairs={{4,0},{8,4},{12,8},{5,1},{9,5},{13,9},{6,2},{10,6},{14,10},{7,3},{... | collective-permute-start | bytes 98312 | tf_op jit(solution)/shard_map/ppermute | solution.py:16
  186.8 4.4 collective-permute-start.27
  188.7 5.2 %collective-permute-start.26 = (bf16[1,1,64,256]{3,2,1,0:T(8,128)(2,1)S(1)}, bf16[1,1,64,256]{3,2,1,0:T(8,128)(2,1)S(1)}, u32[]{:S(2)}, u32[]{:S(2)}) collective-permute-start(bf16[1,1,64,256]{3,2,1,0:T(8,128)(2,1)S(1)} %fusion.120), channel_id=1, source_target_pairs={{0,1},{1,2},{2,3},{4,5},{5,6},{6,7},{8,9},{9,10},{10,11},{12,13},{... | collective-permute-start | bytes 98312 | tf_op jit(solution)/shard_map/ppermute | solution.py:26
  194.0 7.1 %copy-start.15 = (f32[1,256]{1,0:T(1,128)S(1)}, f32[1,256]{1,0:T(1,128)}, u32[]{:S(2)}) copy-start(f32[1,256]{1,0:T(1,128)} %get-tuple-element.99) | copy-start | bytes 3076
  194.0 7.1 %copy-start.16 = (f32[1,256]{1,0:T(1,128)S(1)}, f32[1,256]{1,0:T(1,128)}, u32[]{:S(2)}) copy-start(f32[1,256]{1,0:T(1,128)} %get-tuple-element.109) | copy-start | bytes 3076
  201.2 16.8 %collective-permute-start.15 = (bf16[1,1,64,256]{3,2,1,0:T(8,128)(2,1)S(1)}, bf16[1,1,64,256]{3,2,1,0:T(8,128)(2,1)S(1)}, u32[]{:S(2)}, u32[]{:S(2)}) collective-permute-start(bf16[1,1,64,256]{3,2,1,0:T(8,128)(2,1)S(1)} %get-tuple-element.120), channel_id=1, source_target_pairs={{1,0},{2,1},{3,2},{5,4},{6,5},{7,6},{9,8},{10,9},{11,10},{13,12},{... | collective-permute-start | bytes 98312 | tf_op jit(solution)/shard_map/ppermute | solution.py:27
  203.1 14.9 %collective-permute-start.14 = (bf16[1,1,64,256]{3,2,1,0:T(8,128)(2,1)S(1)}, bf16[1,1,64,256]{3,2,1,0:T(8,128)(2,1)S(1)}, u32[]{:S(2)}, u32[]{:S(2)}) collective-permute-start(bf16[1,1,64,256]{3,2,1,0:T(8,128)(2,1)S(1)} %get-tuple-element.120), channel_id=1, source_target_pairs={{0,1},{1,2},{2,3},{4,5},{5,6},{6,7},{8,9},{9,10},{10,11},{12,13},{... | collective-permute-start | bytes 98312 | tf_op jit(solution)/shard_map/ppermute | solution.py:26
  205.6 7.9 %collective-permute-start.28 = (bf16[1,1,64,256]{3,2,1,0:T(8,128)(2,1)S(1)}, bf16[1,1,64,256]{3,2,1,0:T(8,128)(2,1)S(1)}, u32[]{:S(2)}, u32[]{:S(2)}) collective-permute-start(bf16[1,1,64,256]{3,2,1,0:T(8,128)(2,1)S(1)} %get-tuple-element.119), channel_id=1, source_target_pairs={{4,0},{8,4},{12,8},{5,1},{9,5},{13,9},{6,2},{10,6},{14,10},{7,3},{... | collective-permute-start | bytes 98312 | tf_op jit(solution)/shard_map/ppermute | solution.py:16
  213.5 9.4 %collective-permute-start.31 = (bf16[1,1,64,256]{3,2,1,0:T(8,128)(2,1)S(1)}, bf16[1,1,64,256]{3,2,1,0:T(8,128)(2,1)S(1)}, u32[]{:S(2)}, u32[]{:S(2)}) collective-permute-start(bf16[1,1,64,256]{3,2,1,0:T(8,128)(2,1)S(1)} %fusion.122), channel_id=1, source_target_pairs={{1,0},{2,1},{3,2},{5,4},{6,5},{7,6},{9,8},{10,9},{11,10},{13,12},{... | collective-permute-start | bytes 98312 | tf_op jit(solution)/shard_map/ppermute | solution.py:27
  215.8 7.1 %collective-permute-start.30 = (bf16[1,1,64,256]{3,2,1,0:T(8,128)(2,1)S(1)}, bf16[1,1,64,256]{3,2,1,0:T(8,128)(2,1)S(1)}, u32[]{:S(2)}, u32[]{:S(2)}) collective-permute-start(bf16[1,1,64,256]{3,2,1,0:T(8,128)(2,1)S(1)} %fusion.122), channel_id=1, source_target_pairs={{0,1},{1,2},{2,3},{4,5},{5,6},{6,7},{8,9},{9,10},{10,11},{12,13},{... | collective-permute-start | bytes 98312 | tf_op jit(solution)/shard_map/ppermute | solution.py:26
  224.6 254.4 %all-reduce.24.cloned.1.call-start = ((), (), s32[]{:S(2)}) async-start(), calls=%async_computation | async-start | bytes 5767168 | tf_op jit(solution)/shard_map/psum | solution.py:224
  (14 other events, 19.3 us)
Sparse Core Ops, SparseCore 0:
  224.8 79.7 all-reduce.25
  308.2 170.8 all-reduce.23
